TPU v7x, 512 devices: a whole 4x8x8 slice. The times are simulated.
512 devices in a mesh: shot: 32 (over z, y_hi), dom: 16 (over x, y_lo, core).
Axes of the slice: x: 4, y: 8 (y_hi: 4, y_lo: 2; y = y_hi * 2 + y_lo), z: 8, core: 2. Of those that a mesh axis runs over, the one named last changes fastest.
Arguments:
- coefficient: float32 [512, 16, 384], P('dom'), may hold values from 0.02 to 0.18
- fwd_older: float32 [32, 512, 16, 384], P('shot', 'dom'), may hold values from -6 to 6
- fwd_recent: float32 [32, 512, 16, 384], P('shot', 'dom'), may hold values from -6 to 6
- adj_later: float32 [32, 512, 16, 384], P('shot', 'dom'), may hold values from -6 to 6
- adj_recent: float32 [32, 512, 16, 384], P('shot', 'dom'), may hold values from -6 to 6
- source_xcell: int32 [32], P('shot'), may hold values from 0 to 511
- source_ycell: int32 [32], P('shot'), may hold values from 0 to 15
- source_zcell: int32 [32], P('shot'), may hold values from 0 to 383
- amplitude: float32 [32, 2], P('shot'), may hold values from 3547.24 to 7094.48
- receiver_xcell: int32 [32, 1024], P('shot'), may hold values from 0 to 511
- receiver_ycell: int32 [32, 1024], P('shot'), may hold values from 0 to 15
- receiver_zcell: int32 [32, 1024], P('shot'), may hold values from 0 to 383
- observed: float32 [32, 2, 1024], P('shot'), may hold values from -6 to 6
Outputs:
- fwd_latest: float32 [32, 512, 16, 384], P('shot', 'dom')
- adj_latest: float32 [32, 512, 16, 384], P('shot', 'dom')
- model_gradient: float32 [512, 16, 384], P('dom')
All inputs are finite; a program needn't handle non-finite values.
Results may differ from a plain program's by a relative error of at most 0.0003.
Values sent between devices are 32-bit elements; how exact they have to be, the bound alone decides.
No kernel may reach another device: no remote copies, remote signals or barrier semaphores. Data moves between devices by JAX's collectives and lax.ppermute only.
A program may use at most 64 MiB of HBM per device.

v0:
```python
import jax
import jax.numpy as jnp
from jax import lax
from jax.sharding import PartitionSpec as P

R = 4
stencil_weights = (-205.0 / 72.0, 8.0 / 5.0, -1.0 / 5.0, 8.0 / 315.0, -1.0 / 560.0)


def with_halo(block, sides, width):
    for axis, dim in sides:
        count = lax.axis_size(axis)
        forward = [(i, i + 1) for i in range(count - 1)]
        backward = [(target, source) for source, target in forward]
        low = lax.ppermute(
            lax.slice_in_dim(block, block.shape[dim] - width, None, axis=dim), axis, forward
        )
        high = lax.ppermute(lax.slice_in_dim(block, 0, width, axis=dim), axis, backward)
        block = jnp.concatenate([low, block, high], axis=dim)
    return block


def laplace_core(extended):
    count = extended.shape[0] - 2 * R
    center = extended[R : R + count]
    width_y = center.shape[1]
    width_z = center.shape[2]
    total = 3.0 * stencil_weights[0] * center
    padded = jnp.pad(center, ((0, 0), (R, R), (R, R)))
    for offset in range(1, R + 1):
        weight = stencil_weights[offset]
        total = total + weight * (
            extended[R + offset : R + offset + count] + extended[R - offset : R - offset + count]
        )
        total = total + weight * (
            padded[:, R + offset : R + offset + width_y, R : R + width_z]
            + padded[:, R - offset : R - offset + width_y, R : R + width_z]
        )
        total = total + weight * (
            padded[:, R : R + width_y, R + offset : R + offset + width_z]
            + padded[:, R : R + width_y, R - offset : R - offset + width_z]
        )
    return total


def point_grid(shape, xcells, ycells, zcells, values, start):
    count = shape[0]
    inside = (xcells >= start) & (xcells < start + count)
    local = jnp.clip(xcells - start, 0, count - 1)
    kept = jnp.where(inside, values, jnp.zeros_like(values))
    return jnp.zeros(shape, values.dtype).at[local, ycells, zcells].add(kept)


def sample(field, xcells, ycells, zcells, start):
    count = field.shape[0]
    inside = (xcells >= start) & (xcells < start + count)
    local = jnp.clip(xcells - start, 0, count - 1)
    picked = field[local, ycells, zcells]
    return jnp.where(inside, picked, jnp.zeros_like(picked))


def shards(
    coefficient,
    fwd_older,
    fwd_recent,
    adj_later,
    adj_recent,
    source_xcell,
    source_ycell,
    source_zcell,
    amplitude,
    receiver_xcell,
    receiver_ycell,
    receiver_zcell,
    observed,
):
    count = coefficient.shape[0]
    shape = coefficient.shape
    base = lax.axis_index("dom") * count
    older = fwd_older[0]
    recent = fwd_recent[0]
    later = adj_later[0]
    adj_now = adj_recent[0]
    rxc = receiver_xcell[0]
    ryc = receiver_ycell[0]
    rzc = receiver_zcell[0]

    def advance(current, before, sources):
        extended = with_halo(current, (("dom", 0),), R)
        return 2.0 * current - before + coefficient * (laplace_core(extended) + sources)

    fwd_two = advance(
        recent,
        older,
        point_grid(shape, source_xcell, source_ycell, source_zcell, amplitude[0, 0:1], base),
    )
    fwd_three = advance(
        fwd_two,
        recent,
        point_grid(shape, source_xcell, source_ycell, source_zcell, amplitude[0, 1:2], base),
    )
    samples = jnp.stack(
        [sample(fwd_two, rxc, ryc, rzc, base), sample(fwd_three, rxc, ryc, rzc, base)]
    )
    traces = lax.psum(samples, "dom")
    resid_two = traces[0] - observed[0, 0]
    resid_three = traces[1] - observed[0, 1]
    adj_two = advance(adj_now, later, point_grid(shape, rxc, ryc, rzc, resid_three, base))
    late_term = adj_two * (fwd_three - 2.0 * fwd_two + recent)
    adj_one = advance(adj_two, adj_now, point_grid(shape, rxc, ryc, rzc, resid_two, base))
    early_term = adj_one * (fwd_two - 2.0 * recent + older)
    gradient = lax.psum(early_term + late_term, "shot")
    return (fwd_three[None], adj_one[None], gradient)


def solution(mesh):
    return jax.shard_map(
        shards,
        mesh=mesh,
        in_specs=(
            P("dom", None, None),
            P("shot", "dom", None, None),
            P("shot", "dom", None, None),
            P("shot", "dom", None, None),
            P("shot", "dom", None, None),
            P("shot"),
            P("shot"),
            P("shot"),
            P("shot", None),
            P("shot", None),
            P("shot", None),
            P("shot", None),
            P("shot", None, None),
        ),
        out_specs=(
            P("shot", "dom", None, None),
            P("shot", "dom", None, None),
            P("dom", None, None),
        ),
        check_vma=False,
    )
```

profile of v0, /device:TPU:2, one launch (start us, length us, event | category | flops | bytes accessed | tf_op | source)
XLA Modules:
  0.0 466.0 jit_solution(8528080193020406598)
XLA Ops:
  7.3 1.7 slice_bitcast_fusion.1
  9.0 2.9 collective-permute-start.4
  11.9 1.9 collective-permute-start.5
  14.8 4.5 collective-permute-start
  19.3 1.9 collective-permute-start.1
  28.6 2.7 fusion.80
  34.9 4.5 collective-permute-start.2
  39.4 1.9 collective-permute-start.3
  41.4 2.7 fusion.32
  44.1 10.6 %gather_fusion = f32[1024]{0:T(1024)S(1)} fusion(f32[32,16,384]{2,1,0:T(8,128)S(1)} %fusion.169, s32[1024]{0:T(1024)S(1)} %bitcast.63), kind=kCustom, calls=%fused_computation | custom fusion | bytes 20480 | tf_op jit(solution)/shard_map/gather | solution.py:58
  54.8 3.5 fusion.56
  61.6 1.6 multiply_add_fusion.1
  63.2 10.6 %gather_fusion.1 = f32[1024]{0:T(1024)S(1)} fusion(f32[32,16,384]{2,1,0:T(8,128)S(1)} %multiply_add_fusion.1, s32[1024]{0:T(1024)S(1)} %bitcast.64), kind=kCustom, calls=%fused_computation.1 | custom fusion | bytes 20480 | tf_op jit(solution)/shard_map/gather | solution.py:58
  73.8 25.4 %psum.14 = f32[2,1024]{1,0:T(2,128)S(1)} all-reduce(f32[2,1024]{1,0:T(2,128)S(1)} %pad_maximum_fusion.8), channel_id=1, replica_groups=mesh['shot'=32,'dom'=16] {'dom'}, use_global_device_ids=true, to_apply=%region_1.2 | all-reduce | flops 2048 | bytes 16384 | tf_op jit(solution)/shard_map/psum | solution.py:105
  99.3 6.4 %scatter_fusion = f32[196608]{0:T(1024)S(1)} fusion(f32[196608]{0:T(1024)S(1)} %reshape.178, s32[1024]{0:T(1024)S(1)} %broadcast_select_fusion, f32[1024]{0:T(1024)S(1)} %get-tuple-element.48), kind=kCustom, calls=%fused_computation.2 | custom fusion | flops 1024 | bytes 16384
  106.7 2.0 fusion.168
  108.8 2.5 collective-permute-start.6
  111.3 1.9 collective-permute-start.7
  113.5 5.5 %collective-permute-done.7 = f32[4,16,384]{2,1,0:T(8,128)S(1)} collective-permute-done((f32[4,16,384]{2,1,0:T(8,128)S(1)}, f32[4,16,384]{2,1,0:T(8,128)S(1)}, u32[]{:S(2)}, u32[]{:S(2)}) %collective-permute-start.7) | collective-permute-done | bytes 98336 | tf_op jit(solution)/shard_map/ppermute | solution.py:15
  119.0 3.5 fusion.8
  123.7 6.4 %scatter_fusion.1 = f32[196608]{0:T(1024)S(1)} fusion(f32[196608]{0:T(1024)S(1)} %reshape.182, s32[1024]{0:T(1024)S(1)} %broadcast_select_fusion, f32[1024]{0:T(1024)S(1)} %get-tuple-element.47), kind=kCustom, calls=%fused_computation.3 | custom fusion | flops 1024 | bytes 16384
  131.1 3.6 fusion.171
  134.7 322.4 %all-reduce.6.cloned.1.call-done = f32[32,16,384]{2,1,0:T(8,128)} async-done(((f32[32,16,384]{2,1,0:T(8,128)}), f32[32,16,384]{2,1,0:T(8,128)}) %all-reduce.6.cloned.1.call-update) | async-done | bytes 786448 | tf_op jit(solution)/shard_map/psum | solution.py:112
  457.1 2.1 copy.24
  (63 shorter events, 13.0 us)
Async XLA Ops:
  7.2 18.0 %copy-start.14 = (s32[3]{0:T(128)S(1)}, s32[3]{0:T(128)}, u32[]{:S(2)}) copy-start(s32[3]{0:T(128)} %constant.78.clone.1) | copy-start | bytes 40
  7.2 20.6 %copy-start.12 = (s32[3]{0:T(128)S(1)}, s32[3]{0:T(128)}, u32[]{:S(2)}) copy-start(s32[3]{0:T(128)} %constant.108) | copy-start | bytes 40
  7.2 20.7 %copy-start.13 = (s32[3]{0:T(128)S(1)}, s32[3]{0:T(128)}, u32[]{:S(2)}) copy-start(s32[3]{0:T(128)} %constant.105) | copy-start | bytes 40
  7.2 21.4 %copy-start.1 = (f32[1,32,16,384]{3,2,1,0:T(8,128)S(1)}, f32[1,32,16,384]{3,2,1,0:T(8,128)}, u32[]{:S(2)}) copy-start(f32[1,32,16,384]{3,2,1,0:T(8,128)} %param.19) | copy-start | bytes 2359300
  7.2 16.0 %copy-start.11 = (f32[1,2]{1,0:T(1,128)S(1)}, f32[1,2]{1,0:T(1,128)}, u32[]{:S(2)}) copy-start(f32[1,2]{1,0:T(1,128)} %param.25) | copy-start | bytes 28
  7.2 19.9 %copy-start.7 = (f32[1,2,1024]{2,1,0:T(2,128)S(1)}, f32[1,2,1024]{2,1,0:T(2,128)}, u32[]{:S(2)}) copy-start(f32[1,2,1024]{2,1,0:T(2,128)} %param.29) | copy-start | bytes 24580
  7.2 20.5 %copy-start.5 = (s32[1,1024]{1,0:T(1,128)S(1)}, s32[1,1024]{1,0:T(1,128)}, u32[]{:S(2)}) copy-start(s32[1,1024]{1,0:T(1,128)} %param.26) | copy-start | bytes 12292
  7.2 20.5 %copy-start.9 = (s32[1,1024]{1,0:T(1,128)S(1)}, s32[1,1024]{1,0:T(1,128)}, u32[]{:S(2)}) copy-start(s32[1,1024]{1,0:T(1,128)} %param.28) | copy-start | bytes 12292
  7.3 20.5 %copy-start.8 = (s32[1,1024]{1,0:T(1,128)S(1)}, s32[1,1024]{1,0:T(1,128)}, u32[]{:S(2)}) copy-start(s32[1,1024]{1,0:T(1,128)} %param.27) | copy-start | bytes 12292
  7.3 449.8 %all-reduce.6.cloned.1.call-start = ((), (), s32[]{:S(2)}) async-start(), calls=%async_computation | async-start | bytes 1572864 | tf_op jit(solution)/shard_map/psum | solution.py:112
  9.0 32.4 %collective-permute-start.4 = (f32[4,16,384]{2,1,0:T(8,128)}, f32[4,16,384]{2,1,0:T(8,128)S(1)}, u32[]{:S(2)}, u32[]{:S(2)}) collective-permute-start(f32[4,16,384]{2,1,0:T(8,128)} %get-tuple-element.33), channel_id=1, source_target_pairs={{1,0},{2,1},{3,2},{4,3},{5,4},{6,5},{7,6},{8,7},{9,8},{10,9},{11,1... | collective-permute-start | bytes 294920 | tf_op jit(solution)/shard_map/ppermute | solution.py:18
  11.9 29.5 %collective-permute-start.5 = (f32[4,16,384]{2,1,0:T(8,128)}, f32[4,16,384]{2,1,0:T(8,128)S(1)}, u32[]{:S(2)}, u32[]{:S(2)}) collective-permute-start(f32[4,16,384]{2,1,0:T(8,128)} %get-tuple-element.34), channel_id=1, source_target_pairs={{0,1},{1,2},{2,3},{3,4},{4,5},{5,6},{6,7},{7,8},{8,9},{9,10},{10,1... | collective-permute-start | bytes 294920 | tf_op jit(solution)/shard_map/ppermute | solution.py:15
  14.8 13.9 %collective-permute-start = (f32[4,16,384]{2,1,0:T(8,128)S(1)}, f32[4,16,384]{2,1,0:T(8,128)S(1)}, u32[]{:S(2)}, u32[]{:S(2)}) collective-permute-start(f32[4,16,384]{2,1,0:T(8,128)S(1)} %get-tuple-element.37), channel_id=1, source_target_pairs={{1,0},{2,1},{3,2},{4,3},{5,4},{6,5},{7,6},{8,7},{9,8},{10,9},{11,1... | collective-permute-start | bytes 294920 | tf_op jit(solution)/shard_map/ppermute | solution.py:18
  19.3 9.3 %collective-permute-start.1 = (f32[4,16,384]{2,1,0:T(8,128)S(1)}, f32[4,16,384]{2,1,0:T(8,128)S(1)}, u32[]{:S(2)}, u32[]{:S(2)}) collective-permute-start(f32[4,16,384]{2,1,0:T(8,128)S(1)} %get-tuple-element.38), channel_id=1, source_target_pairs={{0,1},{1,2},{2,3},{3,4},{4,5},{5,6},{6,7},{7,8},{8,9},{9,10},{10,1... | collective-permute-start | bytes 294920 | tf_op jit(solution)/shard_map/ppermute | solution.py:15
  28.6 4.1 copy-start.2
  32.8 8.6 %copy-start.3 = (f32[1,32,16,384]{3,2,1,0:T(8,128)S(1)}, f32[1,32,16,384]{3,2,1,0:T(8,128)}, u32[]{:S(2)}) copy-start(f32[1,32,16,384]{3,2,1,0:T(8,128)} %param.21) | copy-start | bytes 2359300
  34.9 19.9 %collective-permute-start.2 = (f32[4,16,384]{2,1,0:T(8,128)}, f32[4,16,384]{2,1,0:T(8,128)S(1)}, u32[]{:S(2)}, u32[]{:S(2)}) collective-permute-start(f32[4,16,384]{2,1,0:T(8,128)} %get-tuple-element.35), channel_id=1, source_target_pairs={{1,0},{2,1},{3,2},{4,3},{5,4},{6,5},{7,6},{8,7},{9,8},{10,9},{11,1... | collective-permute-start | bytes 294920 | tf_op jit(solution)/shard_map/ppermute | solution.py:18
  39.4 15.3 %collective-permute-start.3 = (f32[4,16,384]{2,1,0:T(8,128)}, f32[4,16,384]{2,1,0:T(8,128)S(1)}, u32[]{:S(2)}, u32[]{:S(2)}) collective-permute-start(f32[4,16,384]{2,1,0:T(8,128)} %get-tuple-element.36), channel_id=1, source_target_pairs={{0,1},{1,2},{2,3},{3,4},{4,5},{5,6},{6,7},{7,8},{8,9},{9,10},{10,1... | collective-permute-start | bytes 294920 | tf_op jit(solution)/shard_map/ppermute | solution.py:15
  63.1 68.0 %copy-start = (f32[32,16,384]{2,1,0:T(8,128)}, f32[32,16,384]{2,1,0:T(8,128)S(1)}, u32[]{:S(2)}) copy-start(f32[32,16,384]{2,1,0:T(8,128)S(1)} %multiply_add_fusion.1) | copy-start | bytes 2359300
  63.1 36.1 %copy-start.6 = (f32[1,1,1024]{2,1,0:T(1,128)S(1)}, f32[1,1,1024]{2,1,0:T(1,128)}, u32[]{:S(2)}) copy-start(f32[1,1,1024]{2,1,0:T(1,128)} %get-tuple-element.40) | copy-start | bytes 12292
  63.2 36.1 %copy-start.10 = (pred[1024]{0:T(1024)(128)(4,1)S(1)}, pred[1024]{0:T(1024)(128)(4,1)}, u32[]{:S(2)}) copy-start(pred[1024]{0:T(1024)(128)(4,1)} %fusion.172) | copy-start | bytes 3076
  108.7 10.3 %copy-start.4 = (f32[32,16,384]{2,1,0:T(8,128)}, f32[32,16,384]{2,1,0:T(8,128)S(1)}, u32[]{:S(2)}) copy-start(f32[32,16,384]{2,1,0:T(8,128)S(1)} %fusion.168) | copy-start | bytes 2359300
  108.8 4.7 %collective-permute-start.6 = (f32[4,16,384]{2,1,0:T(8,128)S(1)}, f32[4,16,384]{2,1,0:T(8,128)S(1)}, u32[]{:S(2)}, u32[]{:S(2)}) collective-permute-start(f32[4,16,384]{2,1,0:T(8,128)S(1)} %get-tuple-element.31), channel_id=1, source_target_pairs={{1,0},{2,1},{3,2},{4,3},{5,4},{6,5},{7,6},{8,7},{9,8},{10,9},{11,1... | collective-permute-start | bytes 294920 | tf_op jit(solution)/shard_map/ppermute | solution.py:18
  111.3 7.7 %collective-permute-start.7 = (f32[4,16,384]{2,1,0:T(8,128)S(1)}, f32[4,16,384]{2,1,0:T(8,128)S(1)}, u32[]{:S(2)}, u32[]{:S(2)}) collective-permute-start(f32[4,16,384]{2,1,0:T(8,128)S(1)} %get-tuple-element.32), channel_id=1, source_target_pairs={{0,1},{1,2},{2,3},{3,4},{4,5},{5,6},{6,7},{7,8},{8,9},{9,10},{10,1... | collective-permute-start | bytes 294920 | tf_op jit(solution)/shard_map/ppermute | solution.py:15
Sparse Core Ops, SparseCore 0:
  134.9 322.1 all-reduce.5
where the time goes:
time: 467 us; the launch traced here: 466 us
  waiting for transfers between devices  328 us (70%)
  other arithmetic  35.3 us (8%)
  local copies, waits for them, and re-layouts  34.5 us (7%)
  blocking collectives  25.4 us (5%)
  starting transfers between devices  22.2 us (5%)
  between operations  20.3 us (4%)
    psum x1, waiting for transfers between devices, shards(): gradient = lax.psum(early_term + late_term, 'shot')  322 us
    psum x1, blocking collectives, shards(): traces = lax.psum(samples, 'dom')  25.4 us
    gather x2, local copies, waits for them, and re-layouts, sample(): picked = field[local, ycells, zcells]  21.1 us
    ppermute x4, starting transfers between devices, with_halo(): lax.ppermute(lax.slice_in_dim(block, 0, width, axis=dim), axis, backward)  14.5 us
    unnamed x5, other arithmetic  12.9 us
    add x4, other arithmetic, laplace_core(): total + weight * (padded[:, R:R + width_y, R + offset:R + offset + width_...  12.4 us
  transfers between devices with their start and end apart: 9, of which 3 were waited for; matrix products, arithmetic and copies ran while one was open for 5% of the time, Pallas kernels for 0%

commit v1 on v0

--- a/solution.py
+++ b/solution.py
@@ -109,7 +109,7 @@
     late_term = adj_two * (fwd_three - 2.0 * fwd_two + recent)
     adj_one = advance(adj_two, adj_now, point_grid(shape, rxc, ryc, rzc, resid_two, base))
     early_term = adj_one * (fwd_two - 2.0 * recent + older)
-    gradient = lax.psum(early_term + late_term, "shot")
+    gradient = jnp.sum(lax.all_gather(early_term + late_term, "shot"), axis=0)
     return (fwd_three[None], adj_one[None], gradient)
 
 

time: 467 us -> 467 us (level)
  the two profiles are of different devices: /device:TPU:2 before, /device:TPU:1 now
where the time goes in v1:
time: 467 us; the launch traced here: 466 us
  waiting for transfers between devices  300 us (64%)
  other arithmetic  58.1 us (12%)
  local copies, waits for them, and re-layouts  33.4 us (7%)
  starting transfers between devices  28.1 us (6%)
  blocking collectives  25.7 us (6%)
  between operations  20.2 us (4%)
    all_gather x1, waiting for transfers between devices, shards(): gradient = jnp.sum(lax.all_gather(early_term + late_term, 'shot'), axis=0)  299 us
    psum x1, blocking collectives, shards(): traces = lax.psum(samples, 'dom')  25.7 us
    add x4, other arithmetic, laplace_core(): total + weight * (padded[:, R:R + width_y, R + offset:R + offset + width_...  21.6 us
    gather x2, local copies, waits for them, and re-layouts, sample(): picked = field[local, ycells, zcells]  21.1 us
    ppermute x4, starting transfers between devices, with_halo(): lax.ppermute(lax.slice_in_dim(block, 0, width, axis=dim), axis, backward)  17.4 us
    unnamed x5, other arithmetic  14.2 us
    ppermute x4, starting transfers between devices, with_halo(): lax.ppermute(lax.slice_in_dim(block, block.shape[dim] - width, None, axis...  10.6 us
    reduce_sum x1, other arithmetic, shards(): gradient = jnp.sum(lax.all_gather(early_term + late_term, 'shot'), axis=0)  10.2 us
  transfers between devices with their start and end apart: 9, of which 3 were waited for; matrix products, arithmetic and copies ran while one was open for 8% of the time, Pallas kernels for 0%

profile of v1, /device:TPU:1, one launch (start us, length us, event | category | flops | bytes accessed | tf_op | source)
XLA Modules:
  0.0 466.1 jit_solution(15795087345799210874)
XLA Ops:
  7.2 1.7 slice_bitcast_fusion.1
  9.0 8.8 %collective-permute-start.4 = (f32[4,16,384]{2,1,0:T(8,128)}, f32[4,16,384]{2,1,0:T(8,128)S(1)}, u32[]{:S(2)}, u32[]{:S(2)}) collective-permute-start(f32[4,16,384]{2,1,0:T(8,128)} %get-tuple-element.33), channel_id=1, source_target_pairs={{1,0},{2,1},{3,2},{4,3},{5,4},{6,5},{7,6},{8,7},{9,8},{10,9},{11,1... | collective-permute-start | bytes 294920 | tf_op jit(solution)/shard_map/ppermute | solution.py:18
  17.7 1.9 collective-permute-start.5
  20.6 2.4 collective-permute-start
  23.0 3.2 collective-permute-start.1
  37.8 12.0 %fusion.80 = f32[32,16,384]{2,1,0:T(8,128)S(1)} fusion(f32[32,16,384]{2,1,0:T(8,128)} %bitcast.68, f32[4,16,384]{2,1,0:T(8,128)S(1)} %collective-permute-done.1, f32[4,16,384]{2,1,0:T(8,128)S(1)} %collective-permute-done), kind=kLoop, calls=%fused_computation.196 | loop fusion | flops 8847360 | bytes 1769472 | tf_op jit(solution)/shard_map/add | solution.py:39
  51.2 1.4 fusion.169
  53.3 1.9 collective-permute-start.2
  55.3 3.6 collective-permute-start.3
  58.9 2.7 fusion.32
  61.7 10.6 %gather_fusion = f32[1024]{0:T(1024)S(1)} fusion(f32[32,16,384]{2,1,0:T(8,128)S(1)} %fusion.169, s32[1024]{0:T(1024)S(1)} %bitcast.64), kind=kCustom, calls=%fused_computation | custom fusion | bytes 20480 | tf_op jit(solution)/shard_map/gather | solution.py:58
  72.3 3.5 fusion.56
  79.1 1.6 multiply_add_fusion.1
  80.7 10.6 %gather_fusion.1 = f32[1024]{0:T(1024)S(1)} fusion(f32[32,16,384]{2,1,0:T(8,128)S(1)} %multiply_add_fusion.1, s32[1024]{0:T(1024)S(1)} %bitcast.65), kind=kCustom, calls=%fused_computation.1 | custom fusion | bytes 20480 | tf_op jit(solution)/shard_map/gather | solution.py:58
  91.3 25.7 %psum.7 = f32[2,1024]{1,0:T(2,128)S(1)} all-reduce(f32[2,1024]{1,0:T(2,128)S(1)} %pad_maximum_fusion.8), channel_id=1, replica_groups=mesh['shot'=32,'dom'=16] {'dom'}, use_global_device_ids=true, to_apply=%region_1.2 | all-reduce | flops 2048 | bytes 16384 | tf_op jit(solution)/shard_map/psum | solution.py:105
  117.1 6.4 %scatter_fusion = f32[196608]{0:T(1024)S(1)} fusion(f32[196608]{0:T(1024)S(1)} %reshape.178, s32[1024]{0:T(1024)S(1)} %broadcast_select_fusion, f32[1024]{0:T(1024)S(1)} %get-tuple-element.48), kind=kCustom, calls=%fused_computation.2 | custom fusion | flops 1024 | bytes 16384
  124.5 2.0 fusion.168
  126.6 4.3 collective-permute-start.6
  130.9 1.9 collective-permute-start.7
  134.5 3.4 fusion.8
  139.1 6.4 %scatter_fusion.1 = f32[196608]{0:T(1024)S(1)} fusion(f32[196608]{0:T(1024)S(1)} %reshape.182, s32[1024]{0:T(1024)S(1)} %broadcast_select_fusion, f32[1024]{0:T(1024)S(1)} %get-tuple-element.47), kind=kCustom, calls=%fused_computation.3 | custom fusion | flops 1024 | bytes 16384
  146.6 3.6 fusion.171
  150.2 298.8 %all-gather.3.cloned.1.call-done = f32[1024,16,384]{2,1,0:T(8,128)} async-done(((f32[32,16,384]{2,1,0:T(8,128)}), f32[1024,16,384]{2,1,0:T(8,128)}) %all-gather.3.cloned.1.call-update) | async-done | bytes 25165840 | tf_op jit(solution)/shard_map/all_gather | solution.py:112
  449.0 10.2 %reduce_sum.9 = f32[32,16,384]{2,1,0:T(8,128)} reduce(f32[32,32,16,384]{3,2,1,0:T(8,128)} %bitcast.67, f32[]{:T(128)} %constant.68.clone.1), dimensions={0}, to_apply=%region_4.5 | reduce | flops 6094848 | bytes 25952260 | tf_op jit(solution)/shard_map/reduce_sum | solution.py:112
  (47 shorter events, 17.2 us)
Async XLA Ops:
  7.2 44.0 %copy-start.1 = (f32[1,32,16,384]{3,2,1,0:T(8,128)S(1)}, f32[1,32,16,384]{3,2,1,0:T(8,128)}, u32[]{:S(2)}) copy-start(f32[1,32,16,384]{3,2,1,0:T(8,128)} %param.19) | copy-start | bytes 2359300
  7.2 44.0 %copy-start.2 = (f32[32,16,384]{2,1,0:T(8,128)S(1)}, f32[32,16,384]{2,1,0:T(8,128)}, u32[]{:S(2)}) copy-start(f32[32,16,384]{2,1,0:T(8,128)} %param.17) | copy-start | bytes 2359300
  7.2 441.8 %all-gather.3.cloned.1.call-start = ((), (), s32[]{:S(2)}) async-start(), calls=%async_computation | async-start | bytes 25952256 | tf_op jit(solution)/shard_map/all_gather | solution.py:112
  9.0 49.9 %collective-permute-start.4 = (f32[4,16,384]{2,1,0:T(8,128)}, f32[4,16,384]{2,1,0:T(8,128)S(1)}, u32[]{:S(2)}, u32[]{:S(2)}) collective-permute-start(f32[4,16,384]{2,1,0:T(8,128)} %get-tuple-element.33), channel_id=1, source_target_pairs={{1,0},{2,1},{3,2},{4,3},{5,4},{6,5},{7,6},{8,7},{9,8},{10,9},{11,1... | collective-permute-start | bytes 294920 | tf_op jit(solution)/shard_map/ppermute | solution.py:18
  17.7 41.2 %collective-permute-start.5 = (f32[4,16,384]{2,1,0:T(8,128)}, f32[4,16,384]{2,1,0:T(8,128)S(1)}, u32[]{:S(2)}, u32[]{:S(2)}) collective-permute-start(f32[4,16,384]{2,1,0:T(8,128)} %get-tuple-element.34), channel_id=1, source_target_pairs={{0,1},{1,2},{2,3},{3,4},{4,5},{5,6},{6,7},{7,8},{8,9},{9,10},{10,1... | collective-permute-start | bytes 294920 | tf_op jit(solution)/shard_map/ppermute | solution.py:15
  20.6 17.2 %collective-permute-start = (f32[4,16,384]{2,1,0:T(8,128)S(1)}, f32[4,16,384]{2,1,0:T(8,128)S(1)}, u32[]{:S(2)}, u32[]{:S(2)}) collective-permute-start(f32[4,16,384]{2,1,0:T(8,128)S(1)} %get-tuple-element.37), channel_id=1, source_target_pairs={{1,0},{2,1},{3,2},{4,3},{5,4},{6,5},{7,6},{8,7},{9,8},{10,9},{11,1... | collective-permute-start | bytes 294920 | tf_op jit(solution)/shard_map/ppermute | solution.py:18
  23.0 14.8 %collective-permute-start.1 = (f32[4,16,384]{2,1,0:T(8,128)S(1)}, f32[4,16,384]{2,1,0:T(8,128)S(1)}, u32[]{:S(2)}, u32[]{:S(2)}) collective-permute-start(f32[4,16,384]{2,1,0:T(8,128)S(1)} %get-tuple-element.38), channel_id=1, source_target_pairs={{0,1},{1,2},{2,3},{3,4},{4,5},{5,6},{6,7},{7,8},{8,9},{9,10},{10,1... | collective-permute-start | bytes 294920 | tf_op jit(solution)/shard_map/ppermute | solution.py:15
  51.2 7.7 %copy-start.3 = (f32[1,32,16,384]{3,2,1,0:T(8,128)S(1)}, f32[1,32,16,384]{3,2,1,0:T(8,128)}, u32[]{:S(2)}) copy-start(f32[1,32,16,384]{3,2,1,0:T(8,128)} %param.21) | copy-start | bytes 2359300
  53.3 19.0 %collective-permute-start.2 = (f32[4,16,384]{2,1,0:T(8,128)}, f32[4,16,384]{2,1,0:T(8,128)S(1)}, u32[]{:S(2)}, u32[]{:S(2)}) collective-permute-start(f32[4,16,384]{2,1,0:T(8,128)} %get-tuple-element.35), channel_id=1, source_target_pairs={{1,0},{2,1},{3,2},{4,3},{5,4},{6,5},{7,6},{8,7},{9,8},{10,9},{11,1... | collective-permute-start | bytes 294920 | tf_op jit(solution)/shard_map/ppermute | solution.py:18
  55.3 17.1 %collective-permute-start.3 = (f32[4,16,384]{2,1,0:T(8,128)}, f32[4,16,384]{2,1,0:T(8,128)S(1)}, u32[]{:S(2)}, u32[]{:S(2)}) collective-permute-start(f32[4,16,384]{2,1,0:T(8,128)} %get-tuple-element.36), channel_id=1, source_target_pairs={{0,1},{1,2},{2,3},{3,4},{4,5},{5,6},{6,7},{7,8},{8,9},{9,10},{10,1... | collective-permute-start | bytes 294920 | tf_op jit(solution)/shard_map/ppermute | solution.py:15
  80.7 65.9 %copy-start = (f32[32,16,384]{2,1,0:T(8,128)}, f32[32,16,384]{2,1,0:T(8,128)S(1)}, u32[]{:S(2)}) copy-start(f32[32,16,384]{2,1,0:T(8,128)S(1)} %multiply_add_fusion.1) | copy-start | bytes 2359300
  80.7 10.6 %copy-start.5 = (s32[1,1024]{1,0:T(1,128)S(1)}, s32[1,1024]{1,0:T(1,128)}, u32[]{:S(2)}) copy-start(s32[1,1024]{1,0:T(1,128)} %param.26) | copy-start | bytes 12292
  80.7 36.4 %copy-start.6 = (pred[1024]{0:T(1024)(128)(4,1)S(1)}, pred[1024]{0:T(1024)(128)(4,1)}, u32[]{:S(2)}) copy-start(pred[1024]{0:T(1024)(128)(4,1)} %fusion.172) | copy-start | bytes 3076
  126.6 7.9 %copy-start.4 = (f32[32,16,384]{2,1,0:T(8,128)}, f32[32,16,384]{2,1,0:T(8,128)S(1)}, u32[]{:S(2)}) copy-start(f32[32,16,384]{2,1,0:T(8,128)S(1)} %fusion.168) | copy-start | bytes 2359300
  126.6 6.8 %collective-permute-start.6 = (f32[4,16,384]{2,1,0:T(8,128)S(1)}, f32[4,16,384]{2,1,0:T(8,128)S(1)}, u32[]{:S(2)}, u32[]{:S(2)}) collective-permute-start(f32[4,16,384]{2,1,0:T(8,128)S(1)} %get-tuple-element.31), channel_id=1, source_target_pairs={{1,0},{2,1},{3,2},{4,3},{5,4},{6,5},{7,6},{8,7},{9,8},{10,9},{11,1... | collective-permute-start | bytes 294920 | tf_op jit(solution)/shard_map/ppermute | solution.py:18
  130.9 3.5 collective-permute-start.7
Sparse Core Ops, SparseCore 0:
  150.3 298.6 all-gather.2
